TPU v7x, 512 devices: a whole 4x8x8 slice. The times are simulated.
512 devices in a mesh: date: 8 (over z), trade: 64 (over x, y, core).
Axes of the slice: x: 4, y: 8, z: 8, core: 2. Of those that a mesh axis runs over, the one named last changes fastest.
Arguments:
- initial_term_structure: float32 [48], replicated, may hold values from 0.01 to 0.06
- long_level: float32 [48], replicated, may hold values from 0.01 to 0.07
- reversion: float32 [48], replicated, may hold values from 0.02 to 2
- volatility: float32 [48], replicated, may hold values from 0.002 to 0.01
- mixing: float32 [48, 48], replicated, may hold values from -0.875 to 0.875
- shocks: float32 [16, 48, 512], P('date'), may hold values from -6 to 6
- cashflows: bfloat16 [48, 524288], P(None, 'trade'), may hold values from -0.01953125 to 0.01953125
- maturity: int32 [524288], P('trade'), may hold values from 1 to 16, as said below
- netting: int32 [524288], P('trade'), may hold values from 0 to 255
Outputs:
- exposure: float32 [16, 256], P('date', 'trade')
Inputs may be any that keep to these rules, and one draw needn't show every extreme that they name: Trades are grouped by maturity along trade: the trades held by one device mature within a narrow band of dates that rises with the device's index.
All inputs are finite; a program needn't handle non-finite values.
Results may differ from a plain program's by a relative error of at most 0.003.
Values may be sent and summed in bfloat16 or wider, within the bound.
No kernel may reach another device: no remote copies, remote signals or barrier semaphores. Data moves between devices by JAX's collectives and lax.ppermute only.
A program may use at most 64 MiB of HBM per device.

v0:
```python
import jax
import jax.numpy as jnp
from jax import lax
from jax.sharding import PartitionSpec as P

SETS_DEV = 4


def from_behind(array, axis, by):
    devices = lax.axis_size(axis)
    pairs = [(i, i + by) for i in range(devices) if 0 <= i + by < devices]
    return lax.ppermute(array, axis, pairs)


def per_device(
    initial_term_structure,
    long_level,
    reversion,
    volatility,
    mixing,
    shocks,
    cashflows,
    maturity,
    netting,
):
    section = shocks.shape[0]
    factors = shocks.shape[1]
    paths = shocks.shape[2]
    sets_all = SETS_DEV * lax.axis_size("trade")
    date_index = lax.axis_index("date")
    decay = jnp.exp(-0.25 * reversion)[:, None]
    drift = ((1.0 - jnp.exp(-0.25 * reversion)) * long_level)[:, None]
    tenor = 0.25 * (jnp.arange(factors, dtype=jnp.float32) + 1.0)
    y_start = jnp.broadcast_to(initial_term_structure[:, None], (factors, paths))
    offsets = []
    powers = []
    running = jnp.zeros((factors, paths), jnp.float32)
    power = jnp.ones((factors, 1), jnp.float32)
    for step in range(section):
        moved = jnp.dot(mixing, shocks[step], precision=lax.Precision.HIGHEST)
        running = decay * running + drift + volatility[:, None] * moved
        power = power * decay
        offsets.append(running)
        powers.append(power)
    segment_multiplier = powers[-1]
    section_shift = offsets[-1]
    incoming_state = y_start
    for round_number in range(lax.axis_size("date") - 1):
        y_leave = segment_multiplier * incoming_state + section_shift
        arrived = from_behind(y_leave.astype(jnp.bfloat16), "date", 1).astype(y_leave.dtype)
        incoming_state = jnp.where(date_index == 0, y_start, arrived)
    discounts = []
    for step in range(section):
        y_now = powers[step] * incoming_state + offsets[step]
        discounts.append(jnp.exp(-y_now * tenor[:, None]).astype(jnp.bfloat16))
    codes = jnp.stack([maturity, netting])
    cash_held, codes_held = (cashflows, codes)
    order = jnp.argsort(-codes_held[0], stable=True)
    cash_held = jnp.take(cash_held, order, axis=1)
    codes_held = jnp.take(codes_held, order, axis=1)
    local_trades = cash_held.shape[1]
    block = min(1024, local_trades)
    blocks = local_trades // block
    set_ids = jnp.arange(sets_all, dtype=jnp.int32)

    def block_data(index):
        start = index * block
        cash_block = lax.dynamic_slice_in_dim(cash_held, start, block, 1)
        code_block = lax.dynamic_slice_in_dim(codes_held, start, block, 1)
        return (cash_block, code_block[0], code_block[1])

    partial_sum_rows = []
    for step in range(section):
        valuation_date = date_index * section + step

        def add_rows(index, running_total):
            cash_block, expiry_tile, set_block = block_data(index)

            def contract_worth(credit_tally):
                weight = jnp.maximum(expiry_tile - valuation_date, 0).astype(
                    jnp.float32
                ) / expiry_tile.astype(jnp.float32)
                rows = cash_block.astype(jnp.float32).T * weight[:, None]
                trade_member = (set_ids[:, None] == set_block[None, :]).astype(jnp.float32)
                return credit_tally + jnp.dot(trade_member, rows, precision=lax.Precision.HIGHEST)

            return lax.cond(
                jnp.max(expiry_tile) > valuation_date,
                contract_worth,
                lambda credit_tally: credit_tally,
                running_total,
            )

        partial_sum_rows.append(
            lax.fori_loop(0, blocks, add_rows, jnp.zeros((sets_all, factors), jnp.float32))
        )
    partial_values = []
    for step in range(section):
        partial_values.append(
            jnp.dot(
                partial_sum_rows[step],
                discounts[step].astype(jnp.float32),
                precision=lax.Precision.HIGHEST,
            )
        )
    owned = lax.psum_scatter(jnp.stack(partial_values), "trade", scatter_dimension=1, tiled=True)
    return jnp.mean(jnp.maximum(owned, 0.0), axis=2)


def solution(mesh):
    return jax.shard_map(
        per_device,
        mesh=mesh,
        in_specs=(
            P(),
            P(),
            P(),
            P(),
            P(),
            P("date", None, None),
            P(None, "trade"),
            P("trade"),
            P("trade"),
        ),
        out_specs=P("date", "trade"),
        check_vma=False,
    )
```

profile of v0, /device:TPU:1, one launch (start us, length us, event | category | flops | bytes accessed | tf_op | source)
XLA Modules:
  0.0 368.7 jit_solution(2612339743787459990)
XLA Ops:
  7.3 1.1 fusion.21
  8.4 1.1 add_convert_fusion.6
  9.5 4.8 %collective-permute-start = (bf16[48,512]{1,0:T(8,128)(2,1)S(1)}, bf16[48,512]{1,0:T(8,128)(2,1)S(1)}, u32[]{:S(2)}, u32[]{:S(2)}) collective-permute-start(bf16[48,512]{1,0:T(8,128)(2,1)S(1)} %get-tuple-element.404), channel_id=1, source_target_pairs={{0,64},{64,128},{128,192},{192,256},{256,320},{320,384},{384,448},... | collective-permute-start | bytes 147464 | tf_op jit(solution)/shard_map/ppermute | solution.py:12
  16.0 6.8 %sort.17 = (s32[8192]{0:T(1024)}, s32[8192]{0:T(1024)S(1)}) sort(s32[8192]{0:T(1024)S(1)} %neg.9, s32[8192]{0:T(1024)S(1)} %iota.16), dimensions={0}, to_apply=%region_0.1 | sort | flops 106496 | bytes 131072 | tf_op jit(solution)/shard_map/jit(argsort)/sort | solution.py:58
  23.5 4.0 %collective-permute-start.1 = (bf16[48,512]{1,0:T(8,128)(2,1)S(1)}, bf16[48,512]{1,0:T(8,128)(2,1)S(1)}, u32[]{:S(2)}, u32[]{:S(2)}) collective-permute-start(bf16[48,512]{1,0:T(8,128)(2,1)S(1)} %add_convert_fusion.5), channel_id=1, source_target_pairs={{0,64},{64,128},{128,192},{192,256},{256,320},{320,384},{384,448},... | collective-permute-start | bytes 147464 | tf_op jit(solution)/shard_map/ppermute | solution.py:12
  27.5 2.6 copy.22
  30.2 29.9 %gather_fusion = s32[8192,2]{1,0:T(8,128)} fusion(s32[2,8192]{0,1:T(8,128)} %copy.22, s32[8192]{0:T(1024)S(1)} %fusion.34), kind=kCustom, calls=%fused_computation | custom fusion | bytes 163840 | tf_op jit(solution)/shard_map/jit(_take)/gather | solution.py:60
  60.1 4.1 %collective-permute-start.2 = (bf16[48,512]{1,0:T(8,128)(2,1)S(1)}, bf16[48,512]{1,0:T(8,128)(2,1)S(1)}, u32[]{:S(2)}, u32[]{:S(2)}) collective-permute-start(bf16[48,512]{1,0:T(8,128)(2,1)S(1)} %add_convert_fusion.4), channel_id=1, source_target_pairs={{0,64},{64,128},{128,192},{192,256},{256,320},{320,384},{384,448},... | collective-permute-start | bytes 147464 | tf_op jit(solution)/shard_map/ppermute | solution.py:12
  64.3 7.5 %select_bitcast_fusion = s32[2,8192]{0,1:T(8,128)} fusion(s32[8192,2]{1,0:T(8,128)} %gather_fusion, pred[8192]{0:T(1024)(128)(4,1)S(1)} %compare_and_fusion), kind=kLoop, calls=%fused_computation.28 | loop fusion | flops 16384 | bytes 139264 | tf_op jit(solution)/shard_map/jit(_take)/select_n | solution.py:60
  71.8 1.0 copy.23
  72.8 29.2 %gather_fusion.1 = bf16[8192,48]{1,0:T(8,128)(2,1)} fusion(bf16[48,8192]{0,1:T(8,128)(2,1)S(1)} %copy.23, s32[8192]{0:T(1024)S(1)} %fusion.34), kind=kCustom, calls=%fused_computation.1 | custom fusion | bytes 1605632 | tf_op jit(solution)/shard_map/jit(_take)/gather | solution.py:59
  102.1 5.2 %collective-permute-start.3 = (bf16[48,512]{1,0:T(8,128)(2,1)S(1)}, bf16[48,512]{1,0:T(8,128)(2,1)S(1)}, u32[]{:S(2)}, u32[]{:S(2)}) collective-permute-start(bf16[48,512]{1,0:T(8,128)(2,1)S(1)} %add_convert_fusion.3), channel_id=1, source_target_pairs={{0,64},{64,128},{128,192},{192,256},{256,320},{320,384},{384,448},... | collective-permute-start | bytes 147464 | tf_op jit(solution)/shard_map/ppermute | solution.py:12
  107.4 5.8 %select_bitcast_fusion.1 = bf16[48,8192]{0,1:T(8,128)(2,1)S(1)} fusion(bf16[8192,48]{1,0:T(8,128)(2,1)} %gather_fusion.1, pred[8192]{0:T(1024)(128)(4,1)S(1)} %compare_and_fusion), kind=kLoop, calls=%fused_computation.29 | loop fusion | flops 393216 | bytes 1581056 | tf_op jit(solution)/shard_map/jit(_take)/select_n | solution.py:59
  113.2 2.8 copy.24
  117.0 3.1 collective-permute-start.4
  120.1 12.0 %while.35 = (s32[]{:T(128)}, f32[256,48]{0,1:T(8,128)S(1)}, s32[2,8192]{1,0:T(2,128)S(1)}, s32[]{:T(128)}, bf16[48,8192]{1,0:T(8,128)(2,1)S(1)}, /*index=5*/s32[]{:T(128)}, s32[]{:T(128)}, s32[]{:T(128)}, s32[]{:T(128)}) while((s32[]{:T(128)}, f32[256,48]{0,1:T(8,128)S(1)}, s32[2,8192]{1,0:T(2,128)S(1)}, s32[]{:T(128)}, ...), condition=%wide.region_10.11_spmd.clone, body=%wide.region_6.10_spmd.clone.sunk | while | flops 151373824 | bytes 248053 | solution.py:95
  132.2 3.1 collective-permute-start.5
  135.3 16.0 %while.34 = (s32[]{:T(128)}, f32[256,48]{0,1:T(8,128)S(1)}, s32[2,8192]{1,0:T(2,128)S(1)}, s32[]{:T(128)}, bf16[48,8192]{1,0:T(8,128)(2,1)S(1)}, /*index=5*/s32[]{:T(128)}, s32[]{:T(128)}, s32[]{:T(128)}, s32[]{:T(128)}) while((s32[]{:T(128)}, f32[256,48]{0,1:T(8,128)S(1)}, s32[2,8192]{1,0:T(2,128)S(1)}, s32[]{:T(128)}, ...), condition=%wide.region_5.6_spmd.clone, body=%wide.region_1.0_spmd.clone.sunk | while | flops 151373824 | bytes 248053 | solution.py:95
  151.5 1.3 collective-permute-start.6
  152.8 1.1 collective-permute-done.6
  154.8 1.1 pad_maximum_fusion
  156.0 1.3 dynamic-slice
  157.9 202.6 %all-reduce.3.cloned.1.call-done = f32[2,256,512]{2,1,0:T(8,128)} async-done(((f32[2,256,512]{2,1,0:T(8,128)}), f32[2,256,512]{2,1,0:T(8,128)}) %all-reduce.3.cloned.1.call-update) | async-done | bytes 1048592
  360.4 0.9 fusion.35
  (121 shorter events, 28.7 us)
Async XLA Ops:
  6.5 0.7 copy-start
  6.5 53.5 %copy-start.2 = (f32[48]{0:T(128)S(1)}, f32[48]{0:T(128)}, u32[]{:S(2)}) copy-start(f32[48]{0:T(128)} %param.17) | copy-start | bytes 580
  6.5 353.9 %all-reduce.3.cloned.1.call-start = ((), (), s32[]{:S(2)}) async-start(), calls=%async_computation | async-start | bytes 2097152
  9.5 13.2 %collective-permute-start = (bf16[48,512]{1,0:T(8,128)(2,1)S(1)}, bf16[48,512]{1,0:T(8,128)(2,1)S(1)}, u32[]{:S(2)}, u32[]{:S(2)}) collective-permute-start(bf16[48,512]{1,0:T(8,128)(2,1)S(1)} %get-tuple-element.404), channel_id=1, source_target_pairs={{0,64},{64,128},{128,192},{192,256},{256,320},{320,384},{384,448},... | collective-permute-start | bytes 147464 | tf_op jit(solution)/shard_map/ppermute | solution.py:12
  23.5 36.5 %collective-permute-start.1 = (bf16[48,512]{1,0:T(8,128)(2,1)S(1)}, bf16[48,512]{1,0:T(8,128)(2,1)S(1)}, u32[]{:S(2)}, u32[]{:S(2)}) collective-permute-start(bf16[48,512]{1,0:T(8,128)(2,1)S(1)} %add_convert_fusion.5), channel_id=1, source_target_pairs={{0,64},{64,128},{128,192},{192,256},{256,320},{320,384},{384,448},... | collective-permute-start | bytes 147464 | tf_op jit(solution)/shard_map/ppermute | solution.py:12
  60.1 11.6 %copy-start.1 = (bf16[48,8192]{1,0:T(8,128)(2,1)S(1)}, bf16[48,8192]{1,0:T(8,128)(2,1)}, u32[]{:S(2)}) copy-start(bf16[48,8192]{1,0:T(8,128)(2,1)} %param.23) | copy-start | bytes 2359300
  60.1 41.9 %collective-permute-start.2 = (bf16[48,512]{1,0:T(8,128)(2,1)S(1)}, bf16[48,512]{1,0:T(8,128)(2,1)S(1)}, u32[]{:S(2)}, u32[]{:S(2)}) collective-permute-start(bf16[48,512]{1,0:T(8,128)(2,1)S(1)} %add_convert_fusion.4), channel_id=1, source_target_pairs={{0,64},{64,128},{128,192},{192,256},{256,320},{320,384},{384,448},... | collective-permute-start | bytes 147464 | tf_op jit(solution)/shard_map/ppermute | solution.py:12
  102.1 14.7 %collective-permute-start.3 = (bf16[48,512]{1,0:T(8,128)(2,1)S(1)}, bf16[48,512]{1,0:T(8,128)(2,1)S(1)}, u32[]{:S(2)}, u32[]{:S(2)}) collective-permute-start(bf16[48,512]{1,0:T(8,128)(2,1)S(1)} %add_convert_fusion.3), channel_id=1, source_target_pairs={{0,64},{64,128},{128,192},{192,256},{256,320},{320,384},{384,448},... | collective-permute-start | bytes 147464 | tf_op jit(solution)/shard_map/ppermute | solution.py:12
  117.0 15.1 %collective-permute-start.4 = (bf16[48,512]{1,0:T(8,128)(2,1)S(1)}, bf16[48,512]{1,0:T(8,128)(2,1)S(1)}, u32[]{:S(2)}, u32[]{:S(2)}) collective-permute-start(bf16[48,512]{1,0:T(8,128)(2,1)S(1)} %add_convert_fusion.2), channel_id=1, source_target_pairs={{0,64},{64,128},{128,192},{192,256},{256,320},{320,384},{384,448},... | collective-permute-start | bytes 147464 | tf_op jit(solution)/shard_map/ppermute | solution.py:12
  132.2 19.2 %collective-permute-start.5 = (bf16[48,512]{1,0:T(8,128)(2,1)S(1)}, bf16[48,512]{1,0:T(8,128)(2,1)S(1)}, u32[]{:S(2)}, u32[]{:S(2)}) collective-permute-start(bf16[48,512]{1,0:T(8,128)(2,1)S(1)} %add_convert_fusion.1), channel_id=1, source_target_pairs={{0,64},{64,128},{128,192},{192,256},{256,320},{320,384},{384,448},... | collective-permute-start | bytes 147464 | tf_op jit(solution)/shard_map/ppermute | solution.py:12
  151.5 2.5 collective-permute-start.6
Sparse Core Ops, SparseCore 0:
  156.1 204.3 all-reduce.2
where the time goes:
time: 370 us; the launch traced here: 369 us
  waiting for transfers between devices  204 us (55%)
  local copies, waits for them, and re-layouts  68 us (18%)
  other arithmetic  37.1 us (10%)
  starting transfers between devices  25.7 us (7%)
  between operations  14.3 us (4%)
  loops' own time  11.3 us (3%)
  matrix products  8.62 us (2%)
    unnamed x2, waiting for transfers between devices  203 us
    gather x1, local copies, waits for them, and re-layouts, per_device(): codes_held = jnp.take(codes_held, order, axis=1)  29.9 us
    gather x1, local copies, waits for them, and re-layouts, per_device(): cash_held = jnp.take(cash_held, order, axis=1)  29.2 us
    ppermute x7, starting transfers between devices, from_behind(): return lax.ppermute(array, axis, pairs)  25.7 us
    reduce_max x16, other arithmetic, add_rows(): jnp.max(expiry_tile) > valuation_date  10.9 us
    another operation x2, loops' own time, per_device(): lax.fori_loop(0, blocks, add_rows, jnp.zeros((sets_all, factors), jnp.flo...  10.8 us
    select_n x1, other arithmetic, per_device(): codes_held = jnp.take(codes_held, order, axis=1)  7.49 us
  transfers between devices with their start and end apart: 8, of which 2 were waited for; matrix products, arithmetic and copies ran while one was open for 29% of the time, Pallas kernels for 0%

commit v1 on v0

v1 whole, which is shorter than its diff:
```python
import jax
import jax.numpy as jnp
from jax import lax
from jax.sharding import PartitionSpec as P

SETS_DEV = 4
RS_MODE = "a2a"
Y_MODE = "permute"


def from_behind(array, axis, by):
    devices = lax.axis_size(axis)
    pairs = [(i, i + by) for i in range(devices) if 0 <= i + by < devices]
    return lax.ppermute(array, axis, pairs)


def per_device(
    initial_term_structure,
    long_level,
    reversion,
    volatility,
    mixing,
    shocks,
    cashflows,
    maturity,
    netting,
):
    section = shocks.shape[0]
    factors = shocks.shape[1]
    paths = shocks.shape[2]
    dates_n = lax.axis_size("date")
    trades_n = lax.axis_size("trade")
    sets_all = SETS_DEV * trades_n
    date_index = lax.axis_index("date")

    trades = cashflows.shape[1]
    mat_f = maturity.astype(jnp.float32)
    weights = []
    for step in range(section):
        valuation_date = date_index * section + step
        weights.append(
            jnp.maximum(maturity - valuation_date, 0).astype(jnp.float32) / mat_f
        )
    cash_f = cashflows.astype(jnp.float32)
    weighted = jnp.concatenate([cash_f * w[None, :] for w in weights], axis=0)
    member = (
        lax.broadcasted_iota(jnp.int32, (sets_all, trades), 0) == netting[None, :]
    ).astype(jnp.bfloat16)
    hi_f = lax.reduce_precision(weighted, exponent_bits=8, mantissa_bits=7)
    hi = hi_f.astype(jnp.bfloat16)
    lo = (weighted - hi_f).astype(jnp.bfloat16)
    dims = (((1,), (1,)), ((), ()))
    rows = lax.dot_general(member, hi, dims, preferred_element_type=jnp.float32)
    rows = rows + lax.dot_general(member, lo, dims, preferred_element_type=jnp.float32)
    if RS_MODE == "scatter":
        owned = lax.psum_scatter(rows, "trade", scatter_dimension=0, tiled=True)
    elif RS_MODE == "a2a":
        parts = rows.reshape(trades_n, SETS_DEV, section * factors)
        got = lax.all_to_all(parts, "trade", 0, 0, tiled=True)
        owned = jnp.sum(got, axis=0)
    else:
        whole = lax.psum(rows, "trade")
        owned = lax.dynamic_slice_in_dim(
            whole, lax.axis_index("trade") * SETS_DEV, SETS_DEV, 0
        )

    decay = jnp.exp(-0.25 * reversion)[:, None]
    drift = ((1.0 - jnp.exp(-0.25 * reversion)) * long_level)[:, None]
    tenor = 0.25 * (jnp.arange(factors, dtype=jnp.float32) + 1.0)
    y_start = jnp.broadcast_to(initial_term_structure[:, None], (factors, paths))
    offsets = []
    powers = []
    running = jnp.zeros((factors, paths), jnp.float32)
    steady = jnp.zeros((factors, 1), jnp.float32)
    power = jnp.ones((factors, 1), jnp.float32)
    for step in range(section):
        moved = jnp.dot(mixing, shocks[step], precision=lax.Precision.HIGHEST)
        running = decay * running + drift + volatility[:, None] * moved
        steady = decay * steady + drift
        power = power * decay
        offsets.append(running)
        powers.append(power)
    multiplier = powers[-1]
    noise = (offsets[-1] - steady).astype(jnp.bfloat16)
    if Y_MODE == "permute":
        arrived = [None] + [
            from_behind(noise, "date", by).astype(jnp.float32)
            for by in range(1, dates_n)
        ]
    else:
        gathered = lax.all_gather(noise, "date", axis=0, tiled=False)
        arrived = [None] + [
            lax.dynamic_index_in_dim(
                gathered, jnp.maximum(date_index - by, 0), 0, keepdims=False
            ).astype(jnp.float32)
            for by in range(1, dates_n)
        ]
    incoming_state = y_start
    for by in range(dates_n - 1, 0, -1):
        stepped = multiplier * incoming_state + (steady + arrived[by])
        incoming_state = jnp.where(by <= date_index, stepped, incoming_state)

    values = []
    for step in range(section):
        y_now = powers[step] * incoming_state + offsets[step]
        discount = jnp.exp(-y_now * tenor[:, None]).astype(jnp.bfloat16).astype(jnp.float32)
        set_rows = owned[:, step * factors:(step + 1) * factors]
        value = jnp.dot(set_rows, discount, precision=lax.Precision.HIGHEST)
        values.append(jnp.mean(jnp.maximum(value, 0.0), axis=1))
    return jnp.stack(values)


def solution(mesh):
    return jax.shard_map(
        per_device,
        mesh=mesh,
        in_specs=(
            P(),
            P(),
            P(),
            P(),
            P(),
            P("date", None, None),
            P(None, "trade"),
            P("trade"),
            P("trade"),
        ),
        out_specs=P("date", "trade"),
        check_vma=False,
    )
```

time: 370 us -> 53.3 us (0.14)
  waiting for transfers between devices: 204 us -> 6.19 us
  local copies, waits for them, and re-layouts: 68 us -> 0.84 us
  other arithmetic: 37.1 us -> 3.85 us
  between operations: 14.3 us -> 0.22 us
  loops' own time: 11.3 us -> 0 us
  starting transfers between devices: 25.7 us -> 35.4 us
    unnamed x2 -> x0, waiting for transfers between devices: 203 us -> none
    gather x2 -> x0, local copies, waits for them, and re-layouts: 59.1 us -> none  [the longest x1 29.9 us: per_device(): codes_held = jnp.take(codes_held, order, axis=1)]
    select_n x2 -> x1, other arithmetic: 13.3 us -> 0.21 us  [per_device(): incoming_state = jnp.where(by <= date_index, stepped, incoming_state)]
    all_to_all x0 -> x1, starting transfers between devices: none -> 11.4 us  [per_device(): got = lax.all_to_all(parts, 'trade', 0, 0, tiled=True)]
    another operation x18 -> x0, loops' own time: 11.3 us -> none  [the longest x2 10.8 us: per_device(): lax.fori_loop(0, blocks, add_rows, jnp.zeros((sets_all, factors), jnp.flo...]
    reduce_max x16 -> x0, other arithmetic: 10.9 us -> none  [add_rows(): jnp.max(expiry_tile) > valuation_date]
    sort x1 -> x0, other arithmetic: 6.76 us -> none  [per_device(): order = jnp.argsort(-codes_held[0], stable=True)]
    unnamed x10 -> x6, local copies, waits for them, and re-layouts: 6.01 us -> 0.09 us
  transfers between devices with their start and end apart: 8 -> 8, of which waited for: 2 -> 2; matrix products, arithmetic and copies ran while one was open for 29% -> 12% of each run, Pallas kernels for 0% -> 0%
where the time goes in v1:
time: 53.3 us; the launch traced here: 52.8 us
  starting transfers between devices  35.4 us (66%)
  matrix products  6.24 us (12%)
  waiting for transfers between devices  6.19 us (12%)
  other arithmetic  3.85 us (7%)
  local copies, waits for them, and re-layouts  0.84 us (2%)
    ppermute x7, starting transfers between devices, from_behind(): return lax.ppermute(array, axis, pairs)  24.1 us
    all_to_all x1, starting transfers between devices, per_device(): got = lax.all_to_all(parts, 'trade', 0, 0, tiled=True)  11.4 us
    all_to_all x1, waiting for transfers between devices, per_device(): got = lax.all_to_all(parts, 'trade', 0, 0, tiled=True)  5.09 us
    dot_general x2, matrix products, per_device(): moved = jnp.dot(mixing, shocks[step], precision=lax.Precision.HIGHEST)  2.24 us
    dot_general x1, matrix products, per_device(): lax.dot_general(member, lo, dims, preferred_element_type=jnp.float32)  1.71 us
    dot_general x1, matrix products, per_device(): rows = lax.dot_general(member, hi, dims, preferred_element_type=jnp.float32)  1.61 us
    mul x1, other arithmetic, per_device(): weighted = jnp.concatenate([cash_f * w[None, :] for w in weights], axis=0)  1.41 us
    ppermute x7, waiting for transfers between devices, from_behind(): return lax.ppermute(array, axis, pairs)  1.1 us
  transfers between devices with their start and end apart: 8, of which 2 were waited for; matrix products, arithmetic and copies ran while one was open for 12% of the time, Pallas kernels for 0%

profile of v1, /device:TPU:1, one launch (start us, length us, event | category | flops | bytes accessed | tf_op | source)
XLA Modules:
  0.0 52.8 jit_solution(1766810056810435440)
XLA Ops:
  0.0 0.7 %multiply_add_fusion = (f32[48]{0:T(128)S(1)}, f32[48]{0:T(128)S(1)}, f32[48]{0:T(128)S(1)}, f32[48]{0:T(128)S(1)}, f32[48]{0:T(128)S(1)}, /*index=5*/f32[48]{0:T(128)S(1)}) fusion(f32[48]{0:T(128)} %param.10, f32[48]{0:T(128)} %param.11, f32[48]{0:T(128)} %param.9), kind=kLoop, calls=%fused_computation.36 | loop fusion | flops 432 | bytes 1728 | tf_op jit(solution)/shard_map/add | solution.py:79
  0.7 0.1 copy-done
  0.8 1.1 %fusion.7 = f32[48,512]{1,0:T(8,128)S(1)} fusion(f32[48,48]{1,0:T(8,128)S(1)} %copy-done, f32[2,48,512]{2,1,0:T(8,128)} %param.14, f32[48]{0:T(128)} %param.12, f32[48]{0:T(128)S(1)} %get-tuple-element.10), kind=kOutput, calls=%fused_computation.14 | convolution fusion | flops 14204928 | bytes 206528 | tf_op jit(solution)/shard_map/dot_general | solution.py:77
  1.9 1.1 %subtract_convert_fusion = (bf16[48,512]{1,0:T(8,128)(2,1)S(1)}, f32[48,512]{1,0:T(8,128)S(1)}) fusion(f32[48]{0:T(128)S(1)} %get-tuple-element.9, f32[48,48]{1,0:T(8,128)S(1)} %copy-done, f32[2,48,512]{2,1,0:T(8,128)} %param.14, f32[48]{0:T(128)} %param.12, f32[48]{0:T(128)S(1)} %get-tuple-element.11, f32[48,512]{1,0:T(8,128)S(1)} %fusion.7, ...), kind=kOutput, calls=%fused_computation.25 | convolution fusion | flops 14303232 | bytes 354368 | tf_op jit(solution)/shard_map/dot_general | solution.py:77
  3.0 11.5 %collective-permute-start = (bf16[48,512]{1,0:T(8,128)(2,1)S(1)}, bf16[48,512]{1,0:T(8,128)(2,1)S(1)}, u32[]{:S(2)}, u32[]{:S(2)}) collective-permute-start(bf16[48,512]{1,0:T(8,128)(2,1)S(1)} %get-tuple-element.15), channel_id=1, source_target_pairs={{0,448},{1,449},{2,450},{3,451},{4,452},{5,453},{6,454},{7,455},{8... | collective-permute-start | bytes 147464 | tf_op jit(solution)/shard_map/ppermute | solution.py:14
  14.5 1.3 %collective-permute-start.1 = (bf16[48,512]{1,0:T(8,128)(2,1)S(1)}, bf16[48,512]{1,0:T(8,128)(2,1)S(1)}, u32[]{:S(2)}, u32[]{:S(2)}) collective-permute-start(bf16[48,512]{1,0:T(8,128)(2,1)S(1)} %get-tuple-element.15), channel_id=1, source_target_pairs={{0,384},{64,448},{1,385},{65,449},{2,386},{66,450},{3,387},{67,451... | collective-permute-start | bytes 147464 | tf_op jit(solution)/shard_map/ppermute | solution.py:14
  15.8 1.3 %collective-permute-start.2 = (bf16[48,512]{1,0:T(8,128)(2,1)S(1)}, bf16[48,512]{1,0:T(8,128)(2,1)S(1)}, u32[]{:S(2)}, u32[]{:S(2)}) collective-permute-start(bf16[48,512]{1,0:T(8,128)(2,1)S(1)} %get-tuple-element.15), channel_id=1, source_target_pairs={{0,320},{64,384},{128,448},{1,321},{65,385},{129,449},{2,322},{66,... | collective-permute-start | bytes 147464 | tf_op jit(solution)/shard_map/ppermute | solution.py:14
  17.1 1.3 %collective-permute-start.3 = (bf16[48,512]{1,0:T(8,128)(2,1)S(1)}, bf16[48,512]{1,0:T(8,128)(2,1)S(1)}, u32[]{:S(2)}, u32[]{:S(2)}) collective-permute-start(bf16[48,512]{1,0:T(8,128)(2,1)S(1)} %get-tuple-element.15), channel_id=1, source_target_pairs={{0,256},{64,320},{128,384},{192,448},{1,257},{65,321},{129,385},{1... | collective-permute-start | bytes 147464 | tf_op jit(solution)/shard_map/ppermute | solution.py:14
  18.4 4.9 %collective-permute-start.4 = (bf16[48,512]{1,0:T(8,128)(2,1)S(1)}, bf16[48,512]{1,0:T(8,128)(2,1)S(1)}, u32[]{:S(2)}, u32[]{:S(2)}) collective-permute-start(bf16[48,512]{1,0:T(8,128)(2,1)S(1)} %get-tuple-element.15), channel_id=1, source_target_pairs={{0,192},{64,256},{128,320},{192,384},{256,448},{1,193},{65,257},{1... | collective-permute-start | bytes 147464 | tf_op jit(solution)/shard_map/ppermute | solution.py:14
  23.3 0.9 %convert_divide_fusion.1 = (f32[8192]{0:T(1024)S(1)}, f32[8192]{0:T(1024)S(1)}) fusion(s32[8192]{0:T(1024)} %param.16, s32[]{:T(128)S(6)} %mul.77, s32[]{:T(128)S(6)} %add.113), kind=kLoop, calls=%fused_computation.29 | loop fusion | flops 73728 | bytes 98312 | tf_op jit(solution)/shard_map/div | solution.py:42
  24.2 1.4 %convert_multiply_fusion.1 = (f32[48,8192]{1,0:T(8,128)S(1)}, f32[48,8192]{1,0:T(8,128)S(1)}) fusion(bf16[48,8192]{1,0:T(8,128)(2,1)} %param.15, f32[8192]{0:T(1024)S(1)} %get-tuple-element.7, f32[8192]{0:T(1024)S(1)} %get-tuple-element.8), kind=kLoop, calls=%fused_computation.10 | loop fusion | flops 1179648 | bytes 3997696 | tf_op jit(solution)/shard_map/mul | solution.py:45
  25.6 1.7 %fusion = f32[256,96]{0,1:T(8,128)S(1)} fusion(s32[8192]{0:T(1024)S(1)} %copy-done.2, f32[48,8192]{1,0:T(8,128)S(1)} %get-tuple-element.6, f32[48,8192]{1,0:T(8,128)S(1)} %get-tuple-element.5), kind=kOutput, calls=%fused_computation.1 | convolution fusion | flops 407896064 | bytes 3276800 | tf_op jit(solution)/shard_map/dot_general | solution.py:54
  27.4 1.6 %fusion.8 = f32[256,96]{0,1:T(8,128)S(1)} fusion(f32[256,96]{0,1:T(8,128)S(1)} %fusion, f32[48,8192]{1,0:T(8,128)S(1)} %get-tuple-element.6, f32[48,8192]{1,0:T(8,128)S(1)} %get-tuple-element.5, s32[8192]{0:T(1024)S(1)} %copy-done.2), kind=kOutput, calls=%fused_computation.15 | convolution fusion | flops 407134208 | bytes 3375104 | tf_op jit(solution)/shard_map/dot_general | solution.py:53
  29.0 0.8 %copy.10 = f32[256,96]{1,0:T(8,128)} copy(f32[256,96]{0,1:T(8,128)S(1)} %fusion.8) | data formatting | bytes 196608 | tf_op jit(solution)/shard_map/add | solution.py:54
  29.7 11.4 %all-to-all-start = ((f32[64,4,96]{2,1,0:T(4,128)}), f32[64,4,96]{2,1,0:T(4,128)S(1)}, u32[]{:S(2)}, u32[]{:S(2)}) async-start(f32[64,4,96]{2,1,0:T(4,128)} %bitcast), calls=%async_computation | async-start | bytes 262144 | tf_op jit(solution)/shard_map/all_to_all | solution.py:59
  41.1 1.3 %collective-permute-start.5 = (bf16[48,512]{1,0:T(8,128)(2,1)S(1)}, bf16[48,512]{1,0:T(8,128)(2,1)S(1)}, u32[]{:S(2)}, u32[]{:S(2)}) collective-permute-start(bf16[48,512]{1,0:T(8,128)(2,1)S(1)} %get-tuple-element.15), channel_id=1, source_target_pairs={{0,128},{64,192},{128,256},{192,320},{256,384},{320,448},{1,129},{... | collective-permute-start | bytes 147464 | tf_op jit(solution)/shard_map/ppermute | solution.py:14
  42.4 2.5 %collective-permute-start.6 = (bf16[48,512]{1,0:T(8,128)(2,1)S(1)}, bf16[48,512]{1,0:T(8,128)(2,1)S(1)}, u32[]{:S(2)}, u32[]{:S(2)}) collective-permute-start(bf16[48,512]{1,0:T(8,128)(2,1)S(1)} %get-tuple-element.15), channel_id=1, source_target_pairs={{0,64},{64,128},{128,192},{192,256},{256,320},{320,384},{384,448},... | collective-permute-start | bytes 147464 | tf_op jit(solution)/shard_map/ppermute | solution.py:14
  45.0 1.1 %collective-permute-done.6 = bf16[48,512]{1,0:T(8,128)(2,1)S(1)} collective-permute-done((bf16[48,512]{1,0:T(8,128)(2,1)S(1)}, bf16[48,512]{1,0:T(8,128)(2,1)S(1)}, u32[]{:S(2)}, u32[]{:S(2)}) %collective-permute-start.6) | collective-permute-done | bytes 49184 | tf_op jit(solution)/shard_map/ppermute | solution.py:14
  46.1 0.2 add_select_fusion
  46.3 5.1 %all-to-all-done = f32[64,4,96]{2,1,0:T(4,128)S(1)} async-done(((f32[64,4,96]{2,1,0:T(4,128)}), f32[64,4,96]{2,1,0:T(4,128)S(1)}, u32[]{:S(2)}, u32[]{:S(2)}) %all-to-all-start) | async-done | bytes 98336 | tf_op jit(solution)/shard_map/all_to_all | solution.py:59
  51.4 0.1 reduce_sum.27
  51.5 0.3 fusion.9
  51.8 0.3 fusion.10
  52.2 0.6 %pad_maximum_fusion.1 = f32[2,4]{1,0:T(2,128)} fusion(f32[1,4]{1,0:T(1,128)S(1)} %get-tuple-element.17, f32[1,4]{1,0:T(1,128)S(1)} %get-tuple-element.18), kind=kLoop, calls=%fused_computation.32 | loop fusion | flops 8 | bytes 64 | tf_op jit(solution)/shard_map/stack | solution.py:110
  (13 shorter events, 0.0 us)
Async XLA Ops:
  0.0 0.8 %copy-start = (f32[48,48]{1,0:T(8,128)S(1)}, f32[48,48]{1,0:T(8,128)}, u32[]{:S(2)}) copy-start(f32[48,48]{1,0:T(8,128)} %param.13) | copy-start | bytes 27652
  3.0 38.1 %collective-permute-start = (bf16[48,512]{1,0:T(8,128)(2,1)S(1)}, bf16[48,512]{1,0:T(8,128)(2,1)S(1)}, u32[]{:S(2)}, u32[]{:S(2)}) collective-permute-start(bf16[48,512]{1,0:T(8,128)(2,1)S(1)} %get-tuple-element.15), channel_id=1, source_target_pairs={{0,448},{1,449},{2,450},{3,451},{4,452},{5,453},{6,454},{7,455},{8... | collective-permute-start | bytes 147464 | tf_op jit(solution)/shard_map/ppermute | solution.py:14
  14.5 27.9 %collective-permute-start.1 = (bf16[48,512]{1,0:T(8,128)(2,1)S(1)}, bf16[48,512]{1,0:T(8,128)(2,1)S(1)}, u32[]{:S(2)}, u32[]{:S(2)}) collective-permute-start(bf16[48,512]{1,0:T(8,128)(2,1)S(1)} %get-tuple-element.15), channel_id=1, source_target_pairs={{0,384},{64,448},{1,385},{65,449},{2,386},{66,450},{3,387},{67,451... | collective-permute-start | bytes 147464 | tf_op jit(solution)/shard_map/ppermute | solution.py:14
  15.8 29.2 %collective-permute-start.2 = (bf16[48,512]{1,0:T(8,128)(2,1)S(1)}, bf16[48,512]{1,0:T(8,128)(2,1)S(1)}, u32[]{:S(2)}, u32[]{:S(2)}) collective-permute-start(bf16[48,512]{1,0:T(8,128)(2,1)S(1)} %get-tuple-element.15), channel_id=1, source_target_pairs={{0,320},{64,384},{128,448},{1,321},{65,385},{129,449},{2,322},{66,... | collective-permute-start | bytes 147464 | tf_op jit(solution)/shard_map/ppermute | solution.py:14
  17.1 27.9 %collective-permute-start.3 = (bf16[48,512]{1,0:T(8,128)(2,1)S(1)}, bf16[48,512]{1,0:T(8,128)(2,1)S(1)}, u32[]{:S(2)}, u32[]{:S(2)}) collective-permute-start(bf16[48,512]{1,0:T(8,128)(2,1)S(1)} %get-tuple-element.15), channel_id=1, source_target_pairs={{0,256},{64,320},{128,384},{192,448},{1,257},{65,321},{129,385},{1... | collective-permute-start | bytes 147464 | tf_op jit(solution)/shard_map/ppermute | solution.py:14
  18.4 26.6 %collective-permute-start.4 = (bf16[48,512]{1,0:T(8,128)(2,1)S(1)}, bf16[48,512]{1,0:T(8,128)(2,1)S(1)}, u32[]{:S(2)}, u32[]{:S(2)}) collective-permute-start(bf16[48,512]{1,0:T(8,128)(2,1)S(1)} %get-tuple-element.15), channel_id=1, source_target_pairs={{0,192},{64,256},{128,320},{192,384},{256,448},{1,193},{65,257},{1... | collective-permute-start | bytes 147464 | tf_op jit(solution)/shard_map/ppermute | solution.py:14
  24.2 1.4 %copy-start.2 = (s32[8192]{0:T(1024)S(1)}, s32[8192]{0:T(1024)}, u32[]{:S(2)}) copy-start(s32[8192]{0:T(1024)} %param.17) | copy-start | bytes 98308
  27.4 18.8 %copy-start.1 = (f32[48]{0:T(128)S(1)}, f32[48]{0:T(128)}, u32[]{:S(2)}) copy-start(f32[48]{0:T(128)} %param.9) | copy-start | bytes 580
  29.7 21.7 %all-to-all-start = ((f32[64,4,96]{2,1,0:T(4,128)}), f32[64,4,96]{2,1,0:T(4,128)S(1)}, u32[]{:S(2)}, u32[]{:S(2)}) async-start(f32[64,4,96]{2,1,0:T(4,128)} %bitcast), calls=%async_computation | async-start | bytes 262144 | tf_op jit(solution)/shard_map/all_to_all | solution.py:59
  41.1 3.9 %collective-permute-start.5 = (bf16[48,512]{1,0:T(8,128)(2,1)S(1)}, bf16[48,512]{1,0:T(8,128)(2,1)S(1)}, u32[]{:S(2)}, u32[]{:S(2)}) collective-permute-start(bf16[48,512]{1,0:T(8,128)(2,1)S(1)} %get-tuple-element.15), channel_id=1, source_target_pairs={{0,128},{64,192},{128,256},{192,320},{256,384},{320,448},{1,129},{... | collective-permute-start | bytes 147464 | tf_op jit(solution)/shard_map/ppermute | solution.py:14
  42.4 3.7 %collective-permute-start.6 = (bf16[48,512]{1,0:T(8,128)(2,1)S(1)}, bf16[48,512]{1,0:T(8,128)(2,1)S(1)}, u32[]{:S(2)}, u32[]{:S(2)}) collective-permute-start(bf16[48,512]{1,0:T(8,128)(2,1)S(1)} %get-tuple-element.15), channel_id=1, source_target_pairs={{0,64},{64,128},{128,192},{192,256},{256,320},{320,384},{384,448},... | collective-permute-start | bytes 147464 | tf_op jit(solution)/shard_map/ppermute | solution.py:14

commit v2 on v1

--- a/solution.py
+++ b/solution.py
@@ -5,7 +5,9 @@
 
 SETS_DEV = 4
 RS_MODE = "a2a"
-Y_MODE = "permute"
+Y_MODE = "scan"
+TRADE_SPLIT = ()
+TRADE_AXES = ("trade",)
 
 
 def from_behind(array, axis, by):
@@ -29,9 +31,11 @@
     factors = shocks.shape[1]
     paths = shocks.shape[2]
     dates_n = lax.axis_size("date")
-    trades_n = lax.axis_size("trade")
+    date_index = lax.axis_index("date")
+    trades_n = 1
+    for axis in TRADE_AXES:
+        trades_n *= lax.axis_size(axis)
     sets_all = SETS_DEV * trades_n
-    date_index = lax.axis_index("date")
 
     trades = cashflows.shape[1]
     mat_f = maturity.astype(jnp.float32)
@@ -55,9 +59,11 @@
     if RS_MODE == "scatter":
         owned = lax.psum_scatter(rows, "trade", scatter_dimension=0, tiled=True)
     elif RS_MODE == "a2a":
-        parts = rows.reshape(trades_n, SETS_DEV, section * factors)
-        got = lax.all_to_all(parts, "trade", 0, 0, tiled=True)
-        owned = jnp.sum(got, axis=0)
+        owned = rows
+        for axis in TRADE_AXES:
+            peers = lax.axis_size(axis)
+            parts = owned.reshape(peers, owned.shape[0] // peers, owned.shape[1])
+            owned = jnp.sum(lax.all_to_all(parts, axis, 0, 0, tiled=True), axis=0)
     else:
         whole = lax.psum(rows, "trade")
         owned = lax.dynamic_slice_in_dim(
@@ -87,6 +93,17 @@
             from_behind(noise, "date", by).astype(jnp.float32)
             for by in range(1, dates_n)
         ]
+    elif Y_MODE == "a2a":
+        sent = jnp.broadcast_to(noise[None], (dates_n,) + noise.shape)
+        got = lax.all_to_all(sent, "date", 0, 0, tiled=True)
+        arrived = [None] + [
+            lax.dynamic_index_in_dim(
+                got, jnp.maximum(date_index - by, 0), 0, keepdims=False
+            ).astype(jnp.float32)
+            for by in range(1, dates_n)
+        ]
+    elif Y_MODE == "scan":
+        arrived = None
     else:
         gathered = lax.all_gather(noise, "date", axis=0, tiled=False)
         arrived = [None] + [
@@ -96,7 +113,20 @@
             for by in range(1, dates_n)
         ]
     incoming_state = y_start
-    for by in range(dates_n - 1, 0, -1):
+    if Y_MODE == "scan":
+        inclusive = noise.astype(jnp.float32)
+        exclusive = jnp.zeros_like(inclusive)
+        by = 1
+        while by < dates_n:
+            far = from_behind(inclusive.astype(jnp.bfloat16), "date", by).astype(jnp.float32)
+            exclusive = exclusive + multiplier ** (by - 1) * far
+            inclusive = inclusive + multiplier ** by * far
+            by *= 2
+        for by in range(dates_n - 1, 0, -1):
+            stepped = multiplier * incoming_state + steady
+            incoming_state = jnp.where(by <= date_index, stepped, incoming_state)
+        incoming_state = incoming_state + exclusive
+    for by in range(dates_n - 1, 0, -1) if Y_MODE != "scan" else ():
         stepped = multiplier * incoming_state + (steady + arrived[by])
         incoming_state = jnp.where(by <= date_index, stepped, incoming_state)
 
@@ -111,6 +141,11 @@
 
 
 def solution(mesh):
+    trade = "trade"
+    if TRADE_SPLIT:
+        devices = mesh.devices.reshape((mesh.devices.shape[0],) + TRADE_SPLIT)
+        mesh = jax.sharding.Mesh(devices, ("date",) + TRADE_AXES)
+        trade = TRADE_AXES
     return jax.shard_map(
         per_device,
         mesh=mesh,
@@ -121,10 +156,10 @@
             P(),
             P(),
             P("date", None, None),
-            P(None, "trade"),
-            P("trade"),
-            P("trade"),
+            P(None, trade),
+            P(trade),
+            P(trade),
         ),
-        out_specs=P("date", "trade"),
+        out_specs=P("date", trade),
         check_vma=False,
     )

time: 53.3 us -> 44 us (0.83)
  starting transfers between devices: 35.4 us -> 29.9 us
  waiting for transfers between devices: 6.19 us -> 2.27 us
    ppermute x7 -> x3, starting transfers between devices: 24.1 us -> 18.6 us  [from_behind(): return lax.ppermute(array, axis, pairs)]
    all_to_all x1, waiting for transfers between devices: 5.09 us -> 2.26 us  [per_device(): owned = jnp.sum(lax.all_to_all(parts, axis, 0, 0, tiled=True), axis=0)]
    ppermute x7 -> x3, waiting for transfers between devices: 1.1 us -> 0.01 us  [from_behind(): return lax.ppermute(array, axis, pairs)]
    add x1 -> x0, other arithmetic: 0.7 us -> none  [per_device(): steady = decay * steady + drift]
  transfers between devices with their start and end apart: 8 -> 4, of which waited for: 2 -> 1; matrix products, arithmetic and copies ran while one was open for 12% -> 15% of each run, Pallas kernels for 0% -> 0%
where the time goes in v2:
time: 44 us; the launch traced here: 43.2 us
  starting transfers between devices  29.9 us (68%)
  matrix products  6.29 us (14%)
  other arithmetic  3.84 us (9%)
  waiting for transfers between devices  2.27 us (5%)
  local copies, waits for them, and re-layouts  0.76 us (2%)
    ppermute x3, starting transfers between devices, from_behind(): return lax.ppermute(array, axis, pairs)  18.6 us
    all_to_all x1, starting transfers between devices, per_device(): owned = jnp.sum(lax.all_to_all(parts, axis, 0, 0, tiled=True), axis=0)  11.3 us
    all_to_all x1, waiting for transfers between devices, per_device(): owned = jnp.sum(lax.all_to_all(parts, axis, 0, 0, tiled=True), axis=0)  2.26 us
    dot_general x2, matrix products, per_device(): moved = jnp.dot(mixing, shocks[step], precision=lax.Precision.HIGHEST)  2.25 us
    dot_general x1, matrix products, per_device(): lax.dot_general(member, lo, dims, preferred_element_type=jnp.float32)  1.71 us
    dot_general x1, matrix products, per_device(): rows = lax.dot_general(member, hi, dims, preferred_element_type=jnp.float32)  1.61 us
    mul x1, other arithmetic, per_device(): weighted = jnp.concatenate([cash_f * w[None, :] for w in weights], axis=0)  1.41 us
  transfers between devices with their start and end apart: 4, of which 1 were waited for; matrix products, arithmetic and copies ran while one was open for 15% of the time, Pallas kernels for 0%

profile of v2, /device:TPU:1, one launch (start us, length us, event | category | flops | bytes accessed | tf_op | source)
XLA Modules:
  0.0 43.2 jit_solution(11758487785662901262)
XLA Ops:
  0.0 0.7 %broadcast_select_fusion.6 = (f32[48]{0:T(128)S(1)}, f32[48]{0:T(128)S(1)}, f32[48]{0:T(128)S(1)}, f32[48]{0:T(128)S(1)}, f32[48]{0:T(128)S(1)}, /*index=5*/f32[48]{0:T(128)S(1)}, f32[48]{0:T(128)S(1)}, f32[48]{0:T(128)S(1)}) fusion(pred[]{:T(512)S(6)} %ge.21, pred[]{:T(512)S(6)} %ge.22, pred[]{:T(512)S(6)} %ge.23, pred[]{:T(512)S(6)} %ge.24, pred[]{:T(512)S(6)} %ge.25, ...), kind=kLoop, calls=%fused_computation.48 | loop fusion | flops 1488 | bytes 2119 | tf_op jit(solution)/shard_map/jit(_where)/select_n | solution.py:127
  0.7 0.0 copy-done
  0.7 1.1 %fusion.7 = f32[48,512]{1,0:T(8,128)S(1)} fusion(f32[48,48]{1,0:T(8,128)S(1)} %copy-done, f32[2,48,512]{2,1,0:T(8,128)} %param.14, f32[48]{0:T(128)} %param.12, f32[48]{0:T(128)S(1)} %get-tuple-element.10), kind=kOutput, calls=%fused_computation.14 | convolution fusion | flops 14204928 | bytes 206528 | tf_op jit(solution)/shard_map/dot_general | solution.py:83
  1.9 1.1 %subtract_convert_fusion = (bf16[48,512]{1,0:T(8,128)(2,1)S(1)}, f32[48,512]{1,0:T(8,128)S(1)}) fusion(f32[48]{0:T(128)S(1)} %get-tuple-element.11, f32[48,48]{1,0:T(8,128)S(1)} %copy-done, f32[2,48,512]{2,1,0:T(8,128)} %param.14, f32[48]{0:T(128)} %param.12, f32[48]{0:T(128)S(1)} %get-tuple-element.12, f32[48,512]{1,0:T(8,128)S(1)} %fusion.7, ...), kind=kOutput, calls=%fused_computation.33 | convolution fusion | flops 14303232 | bytes 354368 | tf_op jit(solution)/shard_map/dot_general | solution.py:83
  3.0 4.8 %collective-permute-start = (bf16[48,512]{1,0:T(8,128)(2,1)S(1)}, bf16[48,512]{1,0:T(8,128)(2,1)S(1)}, u32[]{:S(2)}, u32[]{:S(2)}) collective-permute-start(bf16[48,512]{1,0:T(8,128)(2,1)S(1)} %get-tuple-element.17), channel_id=1, source_target_pairs={{0,64},{64,128},{128,192},{192,256},{256,320},{320,384},{384,448},... | collective-permute-start | bytes 147464 | tf_op jit(solution)/shard_map/ppermute | solution.py:16
  7.8 0.9 %convert_divide_fusion.1 = (f32[8192]{0:T(1024)S(1)}, f32[8192]{0:T(1024)S(1)}) fusion(s32[8192]{0:T(1024)} %param.16, s32[]{:T(128)S(6)} %mul.93, s32[]{:T(128)S(6)} %add.116), kind=kLoop, calls=%fused_computation.38 | loop fusion | flops 73728 | bytes 98312 | tf_op jit(solution)/shard_map/div | solution.py:46
  8.7 0.0 copy-start.1
  8.7 1.4 %convert_multiply_fusion.1 = (f32[48,8192]{1,0:T(8,128)S(1)}, f32[48,8192]{1,0:T(8,128)S(1)}) fusion(bf16[48,8192]{1,0:T(8,128)(2,1)} %param.15, f32[8192]{0:T(1024)S(1)} %get-tuple-element.7, f32[8192]{0:T(1024)S(1)} %get-tuple-element.8), kind=kLoop, calls=%fused_computation.10 | loop fusion | flops 1179648 | bytes 3997696 | tf_op jit(solution)/shard_map/mul | solution.py:49
  10.1 1.7 %fusion = f32[256,96]{0,1:T(8,128)S(1)} fusion(s32[8192]{0:T(1024)S(1)} %copy-done.1, f32[48,8192]{1,0:T(8,128)S(1)} %get-tuple-element.6, f32[48,8192]{1,0:T(8,128)S(1)} %get-tuple-element.5), kind=kOutput, calls=%fused_computation.1 | convolution fusion | flops 407896064 | bytes 3276800 | tf_op jit(solution)/shard_map/dot_general | solution.py:58
  11.8 0.0 collective-permute-done
  11.9 0.1 fusion.20
  11.9 5.8 %collective-permute-start.1 = (bf16[48,512]{1,0:T(8,128)(2,1)S(1)}, bf16[48,512]{1,0:T(8,128)(2,1)S(1)}, u32[]{:S(2)}, u32[]{:S(2)}) collective-permute-start(bf16[48,512]{1,0:T(8,128)(2,1)S(1)} %fusion.20), channel_id=1, source_target_pairs={{0,128},{64,192},{128,256},{192,320},{256,384},{320,448},{1,129},{... | collective-permute-start | bytes 147464 | tf_op jit(solution)/shard_map/ppermute | solution.py:16
  17.8 1.6 %fusion.8 = f32[256,96]{0,1:T(8,128)S(1)} fusion(f32[256,96]{0,1:T(8,128)S(1)} %fusion, f32[48,8192]{1,0:T(8,128)S(1)} %get-tuple-element.6, f32[48,8192]{1,0:T(8,128)S(1)} %get-tuple-element.5, s32[8192]{0:T(1024)S(1)} %copy-done.1), kind=kOutput, calls=%fused_computation.15 | convolution fusion | flops 407134208 | bytes 3375104 | tf_op jit(solution)/shard_map/dot_general | solution.py:57
  19.4 0.7 %copy.10 = f32[256,96]{1,0:T(8,128)} copy(f32[256,96]{0,1:T(8,128)S(1)} %fusion.8) | data formatting | bytes 196608 | tf_op jit(solution)/shard_map/add | solution.py:58
  20.1 11.3 %all-to-all-start = ((f32[64,4,96]{2,1,0:T(4,128)}), f32[64,4,96]{2,1,0:T(4,128)S(1)}, u32[]{:S(2)}, u32[]{:S(2)}) async-start(f32[64,4,96]{2,1,0:T(4,128)} %bitcast), calls=%async_computation | async-start | bytes 262144 | tf_op jit(solution)/shard_map/all_to_all | solution.py:66
  31.5 0.0 collective-permute-done.1
  31.5 0.1 fusion.15
  31.6 7.9 %collective-permute-start.2 = (bf16[48,512]{1,0:T(8,128)(2,1)S(1)}, bf16[48,512]{1,0:T(8,128)(2,1)S(1)}, u32[]{:S(2)}, u32[]{:S(2)}) collective-permute-start(bf16[48,512]{1,0:T(8,128)(2,1)S(1)} %fusion.15), channel_id=1, source_target_pairs={{0,256},{64,320},{128,384},{192,448},{1,257},{65,321},{129,385},{1... | collective-permute-start | bytes 147464 | tf_op jit(solution)/shard_map/ppermute | solution.py:16
  39.6 2.3 %all-to-all-done = f32[64,4,96]{2,1,0:T(4,128)S(1)} async-done(((f32[64,4,96]{2,1,0:T(4,128)}), f32[64,4,96]{2,1,0:T(4,128)S(1)}, u32[]{:S(2)}, u32[]{:S(2)}) %all-to-all-start) | async-done | bytes 98336 | tf_op jit(solution)/shard_map/all_to_all | solution.py:66
  41.8 0.1 reduce_sum.27
  41.9 0.0 collective-permute-done.2
  41.9 0.4 fusion.9
  42.3 0.4 fusion.10
  42.6 0.6 %pad_maximum_fusion.1 = f32[2,4]{1,0:T(2,128)} fusion(f32[1,4]{1,0:T(1,128)S(1)} %get-tuple-element.19, f32[1,4]{1,0:T(1,128)S(1)} %get-tuple-element.20), kind=kLoop, calls=%fused_computation.41 | loop fusion | flops 8 | bytes 64 | tf_op jit(solution)/shard_map/stack | solution.py:140
  (4 shorter events, 0.0 us)
Async XLA Ops:
  0.0 0.7 %copy-start = (f32[48,48]{1,0:T(8,128)S(1)}, f32[48,48]{1,0:T(8,128)}, u32[]{:S(2)}) copy-start(f32[48,48]{1,0:T(8,128)} %param.13) | copy-start | bytes 27652
  3.0 8.8 %collective-permute-start = (bf16[48,512]{1,0:T(8,128)(2,1)S(1)}, bf16[48,512]{1,0:T(8,128)(2,1)S(1)}, u32[]{:S(2)}, u32[]{:S(2)}) collective-permute-start(bf16[48,512]{1,0:T(8,128)(2,1)S(1)} %get-tuple-element.17), channel_id=1, source_target_pairs={{0,64},{64,128},{128,192},{192,256},{256,320},{320,384},{384,448},... | collective-permute-start | bytes 147464 | tf_op jit(solution)/shard_map/ppermute | solution.py:16
  8.7 1.4 %copy-start.1 = (s32[8192]{0:T(1024)S(1)}, s32[8192]{0:T(1024)}, u32[]{:S(2)}) copy-start(s32[8192]{0:T(1024)} %param.17) | copy-start | bytes 98308
  11.9 19.5 %collective-permute-start.1 = (bf16[48,512]{1,0:T(8,128)(2,1)S(1)}, bf16[48,512]{1,0:T(8,128)(2,1)S(1)}, u32[]{:S(2)}, u32[]{:S(2)}) collective-permute-start(bf16[48,512]{1,0:T(8,128)(2,1)S(1)} %fusion.20), channel_id=1, source_target_pairs={{0,128},{64,192},{128,256},{192,320},{256,384},{320,448},{1,129},{... | collective-permute-start | bytes 147464 | tf_op jit(solution)/shard_map/ppermute | solution.py:16
  20.1 21.7 %all-to-all-start = ((f32[64,4,96]{2,1,0:T(4,128)}), f32[64,4,96]{2,1,0:T(4,128)S(1)}, u32[]{:S(2)}, u32[]{:S(2)}) async-start(f32[64,4,96]{2,1,0:T(4,128)} %bitcast), calls=%async_computation | async-start | bytes 262144 | tf_op jit(solution)/shard_map/all_to_all | solution.py:66
  31.6 10.3 %collective-permute-start.2 = (bf16[48,512]{1,0:T(8,128)(2,1)S(1)}, bf16[48,512]{1,0:T(8,128)(2,1)S(1)}, u32[]{:S(2)}, u32[]{:S(2)}) collective-permute-start(bf16[48,512]{1,0:T(8,128)(2,1)S(1)} %fusion.15), channel_id=1, source_target_pairs={{0,256},{64,320},{128,384},{192,448},{1,257},{65,321},{129,385},{1... | collective-permute-start | bytes 147464 | tf_op jit(solution)/shard_map/ppermute | solution.py:16

commit v3 on v2

--- a/solution.py
+++ b/solution.py
@@ -6,6 +6,7 @@
 SETS_DEV = 4
 RS_MODE = "a2a"
 Y_MODE = "scan"
+ORDER_TIE = False
 TRADE_SPLIT = ()
 TRADE_AXES = ("trade",)
 
@@ -54,15 +55,31 @@
     hi = hi_f.astype(jnp.bfloat16)
     lo = (weighted - hi_f).astype(jnp.bfloat16)
     dims = (((1,), (1,)), ((), ()))
-    rows = lax.dot_general(member, hi, dims, preferred_element_type=jnp.float32)
-    rows = rows + lax.dot_general(member, lo, dims, preferred_element_type=jnp.float32)
+    both = lax.dot_general(
+        member, jnp.concatenate([hi, lo], axis=0), dims, preferred_element_type=jnp.float32
+    )
+    rows = both[:, : hi.shape[0]] + both[:, hi.shape[0]:]
     if RS_MODE == "scatter":
         owned = lax.psum_scatter(rows, "trade", scatter_dimension=0, tiled=True)
+    elif RS_MODE == "pair":
+        chips_axis, core_axis = TRADE_AXES
+        chips = lax.axis_size(chips_axis)
+        core = lax.axis_index(core_axis)
+        by_core = rows.reshape(chips, 2, SETS_DEV, rows.shape[1])
+        keep = lax.dynamic_index_in_dim(by_core, core, 1, keepdims=False)
+        give = lax.dynamic_index_in_dim(by_core, 1 - core, 1, keepdims=False)
+        mine = keep + lax.ppermute(give, core_axis, [(0, 1), (1, 0)])
+        owned = jnp.sum(lax.all_to_all(mine, chips_axis, 0, 0, tiled=True), axis=0)
     elif RS_MODE == "a2a":
         owned = rows
         for axis in TRADE_AXES:
             peers = lax.axis_size(axis)
             parts = owned.reshape(peers, owned.shape[0] // peers, owned.shape[1])
+            if ORDER_TIE == "rows_first":
+                parts, shocks = lax.optimization_barrier((parts, shocks))
+            if ORDER_TIE == "scan_first":
+                owned = parts
+                break
             owned = jnp.sum(lax.all_to_all(parts, axis, 0, 0, tiled=True), axis=0)
     else:
         whole = lax.psum(rows, "trade")
@@ -126,6 +143,9 @@
             stepped = multiplier * incoming_state + steady
             incoming_state = jnp.where(by <= date_index, stepped, incoming_state)
         incoming_state = incoming_state + exclusive
+        if ORDER_TIE == "scan_first" and RS_MODE == "a2a":
+            parts, incoming_state = lax.optimization_barrier((owned, incoming_state))
+            owned = jnp.sum(lax.all_to_all(parts, TRADE_AXES[0], 0, 0, tiled=True), axis=0)
     for by in range(dates_n - 1, 0, -1) if Y_MODE != "scan" else ():
         stepped = multiplier * incoming_state + (steady + arrived[by])
         incoming_state = jnp.where(by <= date_index, stepped, incoming_state)
@@ -143,7 +163,8 @@
 def solution(mesh):
     trade = "trade"
     if TRADE_SPLIT:
-        devices = mesh.devices.reshape((mesh.devices.shape[0],) + TRADE_SPLIT)
+        split = (mesh.devices.shape[1] // 2, 2) if TRADE_SPLIT == "pair" else TRADE_SPLIT
+        devices = mesh.devices.reshape((mesh.devices.shape[0],) + split)
         mesh = jax.sharding.Mesh(devices, ("date",) + TRADE_AXES)
         trade = TRADE_AXES
     return jax.shard_map(

time: 44 us -> 43.3 us (0.984)
  the two profiles are of different devices: /device:TPU:1 before, /device:TPU:65 now
where the time goes in v3:
time: 43.3 us; the launch traced here: 42.8 us
  starting transfers between devices  26.1 us (60%)
  waiting for transfers between devices  6.47 us (15%)
  matrix products  4.69 us (11%)
  other arithmetic  4.36 us (10%)
  local copies, waits for them, and re-layouts  0.99 us (2%)
    ppermute x3, starting transfers between devices, from_behind(): return lax.ppermute(array, axis, pairs)  14.8 us
    all_to_all x1, starting transfers between devices, per_device(): owned = jnp.sum(lax.all_to_all(parts, axis, 0, 0, tiled=True), axis=0)  11.4 us
    all_to_all x1, waiting for transfers between devices, per_device(): owned = jnp.sum(lax.all_to_all(parts, axis, 0, 0, tiled=True), axis=0)  6.46 us
    dot_general x2, matrix products, per_device(): moved = jnp.dot(mixing, shocks[step], precision=lax.Precision.HIGHEST)  2.24 us
    dot_general x1, matrix products, per_device(): lax.dot_general(member, jnp.concatenate([hi, lo], axis=0), dims, preferre...  1.72 us
    mul x1, other arithmetic, per_device(): weighted = jnp.concatenate([cash_f * w[None, :] for w in weights], axis=0)  1.41 us
  transfers between devices with their start and end apart: 4, of which 1 were waited for; matrix products, arithmetic and copies ran while one was open for 13% of the time, Pallas kernels for 0%

profile of v3, /device:TPU:65, one launch (start us, length us, event | category | flops | bytes accessed | tf_op | source)
XLA Modules:
  0.0 42.8 jit_solution(6472843456838697140)
XLA Ops:
  0.0 0.7 %broadcast_select_fusion.6 = (f32[48]{0:T(128)S(1)}, f32[48]{0:T(128)S(1)}, f32[48]{0:T(128)S(1)}, f32[48]{0:T(128)S(1)}, f32[48]{0:T(128)S(1)}, /*index=5*/f32[48]{0:T(128)S(1)}, f32[48]{0:T(128)S(1)}, f32[48]{0:T(128)S(1)}) fusion(pred[]{:T(512)S(6)} %ge.21, pred[]{:T(512)S(6)} %ge.22, pred[]{:T(512)S(6)} %ge.23, pred[]{:T(512)S(6)} %ge.24, pred[]{:T(512)S(6)} %ge.25, ...), kind=kLoop, calls=%fused_computation.49 | loop fusion | flops 1488 | bytes 2119 | tf_op jit(solution)/shard_map/jit(_where)/select_n | solution.py:144
  0.7 0.0 copy-done
  0.7 1.1 %fusion.7 = f32[48,512]{1,0:T(8,128)S(1)} fusion(f32[48,48]{1,0:T(8,128)S(1)} %copy-done, f32[2,48,512]{2,1,0:T(8,128)} %param.14, f32[48]{0:T(128)} %param.12, f32[48]{0:T(128)S(1)} %get-tuple-element.12), kind=kOutput, calls=%fused_computation.15 | convolution fusion | flops 14204928 | bytes 206528 | tf_op jit(solution)/shard_map/dot_general | solution.py:100
  1.9 1.1 %subtract_convert_fusion = (bf16[48,512]{1,0:T(8,128)(2,1)S(1)}, f32[48,512]{1,0:T(8,128)S(1)}) fusion(f32[48]{0:T(128)S(1)} %get-tuple-element.13, f32[48,48]{1,0:T(8,128)S(1)} %copy-done, f32[2,48,512]{2,1,0:T(8,128)} %param.14, f32[48]{0:T(128)} %param.12, f32[48]{0:T(128)S(1)} %get-tuple-element.14, f32[48,512]{1,0:T(8,128)S(1)} %fusion.7, ...), kind=kOutput, calls=%fused_computation.34 | convolution fusion | flops 14303232 | bytes 354368 | tf_op jit(solution)/shard_map/dot_general | solution.py:100
  3.0 4.0 %collective-permute-start = (bf16[48,512]{1,0:T(8,128)(2,1)S(1)}, bf16[48,512]{1,0:T(8,128)(2,1)S(1)}, u32[]{:S(2)}, u32[]{:S(2)}) collective-permute-start(bf16[48,512]{1,0:T(8,128)(2,1)S(1)} %get-tuple-element.19), channel_id=1, source_target_pairs={{0,64},{64,128},{128,192},{192,256},{256,320},{320,384},{384,448},... | collective-permute-start | bytes 147464 | tf_op jit(solution)/shard_map/ppermute | solution.py:17
  7.0 0.9 %convert_divide_fusion.1 = (f32[8192]{0:T(1024)S(1)}, f32[8192]{0:T(1024)S(1)}) fusion(s32[8192]{0:T(1024)} %param.16, s32[]{:T(128)S(6)} %mul.93, s32[]{:T(128)S(6)} %add.116), kind=kLoop, calls=%fused_computation.39 | loop fusion | flops 73728 | bytes 98312 | tf_op jit(solution)/shard_map/div | solution.py:47
  7.9 1.4 %convert_multiply_fusion.1 = (f32[48,8192]{1,0:T(8,128)S(1)}, f32[48,8192]{1,0:T(8,128)S(1)}) fusion(bf16[48,8192]{1,0:T(8,128)(2,1)} %param.15, f32[8192]{0:T(1024)S(1)} %get-tuple-element.9, f32[8192]{0:T(1024)S(1)} %get-tuple-element.10), kind=kLoop, calls=%fused_computation.11 | loop fusion | flops 1179648 | bytes 3997696 | tf_op jit(solution)/shard_map/mul | solution.py:50
  9.3 0.0 copy-start.1
  9.3 0.5 %reduce-precision_convert_fusion = (bf16[96,8192]{1,0:T(8,128)(2,1)S(1)}, bf16[96,8192]{1,0:T(8,128)(2,1)S(1)}) fusion(f32[48,8192]{1,0:T(8,128)S(1)} %get-tuple-element.8, f32[48,8192]{1,0:T(8,128)S(1)} %get-tuple-element.7), kind=kLoop, calls=%fused_computation.3 | loop fusion | flops 3932160 | bytes 6291456 | tf_op jit(solution)/shard_map/convert_element_type | solution.py:55
  9.8 0.2 copy-done.1
  10.0 1.7 %fusion = f32[256,192]{0,1:T(8,128)S(1)} fusion(s32[8192]{0:T(1024)S(1)} %copy-done.1, bf16[96,8192]{1,0:T(8,128)(2,1)S(1)} %get-tuple-element.6, bf16[96,8192]{1,0:T(8,128)(2,1)S(1)} %get-tuple-element.5), kind=kOutput, calls=%fused_computation.1 | convolution fusion | flops 813694976 | bytes 3375104 | tf_op jit(solution)/shard_map/dot_general | solution.py:58
  11.8 0.0 collective-permute-done
  11.8 0.1 fusion.19
  11.9 7.0 %collective-permute-start.1 = (bf16[48,512]{1,0:T(8,128)(2,1)S(1)}, bf16[48,512]{1,0:T(8,128)(2,1)S(1)}, u32[]{:S(2)}, u32[]{:S(2)}) collective-permute-start(bf16[48,512]{1,0:T(8,128)(2,1)S(1)} %fusion.19), channel_id=1, source_target_pairs={{0,128},{64,192},{128,256},{192,320},{256,384},{320,448},{1,129},{... | collective-permute-start | bytes 147464 | tf_op jit(solution)/shard_map/ppermute | solution.py:17
  18.9 0.8 %copy.10 = f32[256,96]{1,0:T(8,128)} copy(f32[256,96]{0,1:T(8,128)S(1)} %slice_add_fusion) | data formatting | bytes 196608 | tf_op jit(solution)/shard_map/add | solution.py:61
  19.7 11.4 %all-to-all-start = ((f32[64,4,96]{2,1,0:T(4,128)}), f32[64,4,96]{2,1,0:T(4,128)S(1)}, u32[]{:S(2)}, u32[]{:S(2)}) async-start(f32[64,4,96]{2,1,0:T(4,128)} %bitcast), calls=%async_computation | async-start | bytes 262144 | tf_op jit(solution)/shard_map/all_to_all | solution.py:83
  31.0 0.1 fusion.14
  31.1 3.7 %collective-permute-start.2 = (bf16[48,512]{1,0:T(8,128)(2,1)S(1)}, bf16[48,512]{1,0:T(8,128)(2,1)S(1)}, u32[]{:S(2)}, u32[]{:S(2)}) collective-permute-start(bf16[48,512]{1,0:T(8,128)(2,1)S(1)} %fusion.14), channel_id=1, source_target_pairs={{0,256},{64,320},{128,384},{192,448},{1,257},{65,321},{129,385},{1... | collective-permute-start | bytes 147464 | tf_op jit(solution)/shard_map/ppermute | solution.py:17
  34.9 6.5 %all-to-all-done = f32[64,4,96]{2,1,0:T(4,128)S(1)} async-done(((f32[64,4,96]{2,1,0:T(4,128)}), f32[64,4,96]{2,1,0:T(4,128)S(1)}, u32[]{:S(2)}, u32[]{:S(2)}) %all-to-all-start) | async-done | bytes 98336 | tf_op jit(solution)/shard_map/all_to_all | solution.py:83
  41.4 0.1 reduce_sum.27
  41.4 0.0 collective-permute-done.2
  41.4 0.4 fusion.8
  41.8 0.4 fusion.9
  42.2 0.6 %pad_maximum_fusion.1 = f32[2,4]{1,0:T(2,128)} fusion(f32[1,4]{1,0:T(1,128)S(1)} %get-tuple-element.21, f32[1,4]{1,0:T(1,128)S(1)} %get-tuple-element.22), kind=kLoop, calls=%fused_computation.42 | loop fusion | flops 8 | bytes 64 | tf_op jit(solution)/shard_map/stack | solution.py:160
  (5 shorter events, 0.0 us)
Async XLA Ops:
  0.0 0.7 %copy-start = (f32[48,48]{1,0:T(8,128)S(1)}, f32[48,48]{1,0:T(8,128)}, u32[]{:S(2)}) copy-start(f32[48,48]{1,0:T(8,128)} %param.13) | copy-start | bytes 27652
  3.0 8.8 %collective-permute-start = (bf16[48,512]{1,0:T(8,128)(2,1)S(1)}, bf16[48,512]{1,0:T(8,128)(2,1)S(1)}, u32[]{:S(2)}, u32[]{:S(2)}) collective-permute-start(bf16[48,512]{1,0:T(8,128)(2,1)S(1)} %get-tuple-element.19), channel_id=1, source_target_pairs={{0,64},{64,128},{128,192},{192,256},{256,320},{320,384},{384,448},... | collective-permute-start | bytes 147464 | tf_op jit(solution)/shard_map/ppermute | solution.py:17
  9.3 0.8 %copy-start.1 = (s32[8192]{0:T(1024)S(1)}, s32[8192]{0:T(1024)}, u32[]{:S(2)}) copy-start(s32[8192]{0:T(1024)} %param.17) | copy-start | bytes 98308
  11.9 19.2 %collective-permute-start.1 = (bf16[48,512]{1,0:T(8,128)(2,1)S(1)}, bf16[48,512]{1,0:T(8,128)(2,1)S(1)}, u32[]{:S(2)}, u32[]{:S(2)}) collective-permute-start(bf16[48,512]{1,0:T(8,128)(2,1)S(1)} %fusion.19), channel_id=1, source_target_pairs={{0,128},{64,192},{128,256},{192,320},{256,384},{320,448},{1,129},{... | collective-permute-start | bytes 147464 | tf_op jit(solution)/shard_map/ppermute | solution.py:17
  19.7 21.7 %all-to-all-start = ((f32[64,4,96]{2,1,0:T(4,128)}), f32[64,4,96]{2,1,0:T(4,128)S(1)}, u32[]{:S(2)}, u32[]{:S(2)}) async-start(f32[64,4,96]{2,1,0:T(4,128)} %bitcast), calls=%async_computation | async-start | bytes 262144 | tf_op jit(solution)/shard_map/all_to_all | solution.py:83
  31.1 10.3 %collective-permute-start.2 = (bf16[48,512]{1,0:T(8,128)(2,1)S(1)}, bf16[48,512]{1,0:T(8,128)(2,1)S(1)}, u32[]{:S(2)}, u32[]{:S(2)}) collective-permute-start(bf16[48,512]{1,0:T(8,128)(2,1)S(1)} %fusion.14), channel_id=1, source_target_pairs={{0,256},{64,320},{128,384},{192,448},{1,257},{65,321},{129,385},{1... | collective-permute-start | bytes 147464 | tf_op jit(solution)/shard_map/ppermute | solution.py:17
